TPU v7x, 256 devices: a whole 4x4x8 slice. The times are simulated.
256 devices in a mesh: blk: 64 (over z, x_lo, y), circ: 4 (over x_hi, core).
Axes of the slice: x: 4 (x_hi: 2, x_lo: 2; x = x_hi * 2 + x_lo), y: 4, z: 8, core: 2. Of those that a mesh axis runs over, the one named last changes fastest.
Arguments:
- panels: float32 [4, 8192], P(None, ('blk', 'circ')), may hold values from -2 to 2, as said below
- node_of_panel: int32 [8192], P(('blk', 'circ')), may hold values from 0 to 2047, as said below
- stiffener_rows: int32 [32], replicated, may hold values from 0 to 511
- density_start: float32 [16, 8192], P(None, ('blk', 'circ')), may hold values from -6 to 6
- motion_start: float32 [16, 512, 1024], P(None, 'blk', 'circ'), may hold values from -6 to 6
- force: float32 [16, 512, 1024], P(None, 'blk', 'circ'), may hold values from -128 to 128
- stiffness: float32 [512, 1024], P('blk', 'circ'), may hold values from 0.5 to 2
Outputs:
- source_density: float32 [16, 8192], P(None, ('blk', 'circ'))
- surface_pressure: float32 [16, 8192], P(None, ('blk', 'circ'))
- shell_motion: float32 [16, 512, 1024], P(None, 'blk', 'circ')
Inputs may be any that keep to these rules, and one draw needn't show every extreme that they name: `panels`: every panel lies between 0.98 and 1.02 from the z axis, with z between -2 and 2 and area between 0.5 and 2 times 8 pi / 8192. `node_of_panel`: counted as row * 256 + column within the tile of the device that holds the panel. `stiffener_rows`: A row may be listed more than once.
All inputs are finite; a program needn't handle non-finite values.
Results may differ from a plain program's by a relative error of at most 0.0029.
Values may be sent and summed in bfloat16 or wider, within the bound.
No kernel may reach another device: no remote copies, remote signals or barrier semaphores. Data moves between devices by JAX's collectives and lax.ppermute only.
A program may use at most 64 MiB of HBM per device.

v0:
```python
import math
import jax
import jax.numpy as jnp
from jax import lax
from jax.sharding import PartitionSpec as P

ITERS = 4
SWEEPS = 2
wave_number = 4.0
single_scale = 30.0
double_scale = 6.0
hoop_spring = 40.0
inertia_term = 4.0
loss_factor = 0.2
relaxation = 0.3


def padded(block, sides, width):
    for axis, dim in sides:
        count = lax.axis_size(axis)
        forward = [(i, i + 1) for i in range(count - 1)]
        forward.append((count - 1, 0))
        backward = [(target, source) for source, target in forward]
        low = lax.ppermute(
            lax.slice_in_dim(block, block.shape[dim] - width, None, axis=dim), axis, forward
        )
        high = lax.ppermute(lax.slice_in_dim(block, 0, width, axis=dim), axis, backward)
        block = jnp.concatenate([low, block, high], axis=dim)
    return block


def kernel_blocks(targets, sources):
    radial = jnp.sqrt(targets[0] * targets[0] + targets[1] * targets[1])
    normal_x = (targets[0] / radial)[:, None]
    normal_y = (targets[1] / radial)[:, None]
    delta_x = targets[0][:, None] - sources[0][None, :]
    delta_y = targets[1][:, None] - sources[1][None, :]
    delta_z = targets[2][:, None] - sources[2][None, :]
    areas = sources[3][None, :]
    dist_sq = delta_x * delta_x + delta_y * delta_y + delta_z * delta_z + areas / math.pi
    distance = jnp.sqrt(dist_sq)
    inverse = 1.0 / distance
    phase_arg = wave_number * distance
    cosine = jnp.cos(phase_arg)
    sine_part = jnp.sin(phase_arg)
    weight = areas * (1.0 / (4.0 * math.pi)) * inverse
    single = single_scale * weight
    double = double_scale * weight * (normal_x * delta_x + normal_y * delta_y) * inverse * inverse
    real_stack = jnp.concatenate(
        [single * cosine, double * (-cosine - phase_arg * sine_part)], axis=0
    )
    imag_stack = jnp.concatenate(
        [single * sine_part, double * (phase_arg * cosine - sine_part)], axis=0
    )
    return (real_stack.astype(jnp.bfloat16), imag_stack.astype(jnp.bfloat16))


def form_kernels(targets, sources):
    width = sources.shape[1]
    block_cols = math.gcd(width, 1024)
    block_count = width // block_cols
    source_blocks = jnp.transpose(sources.reshape(4, block_count, block_cols), (1, 0, 2))
    real_blocks, imag_blocks = lax.map(lambda block: kernel_blocks(targets, block), source_blocks)
    rows_out = real_blocks.shape[1]
    real_stack = jnp.transpose(real_blocks, (1, 0, 2)).reshape(rows_out, width)
    imag_stack = jnp.transpose(imag_blocks, (1, 0, 2)).reshape(rows_out, width)
    return (real_stack, imag_stack)


def fold_columns(real_stack, imag_stack):

    def fold_step(running, shard_piece, first_col):
        half = shard_piece.shape[0] // 2
        rotated = jnp.concatenate([-shard_piece[half:], shard_piece[:half]], axis=0)
        first = jnp.einsum("lc,rc->lr", shard_piece, real_stack, preferred_element_type=jnp.float32)
        second = jnp.einsum("lc,rc->lr", rotated, imag_stack, preferred_element_type=jnp.float32)
        return first + second

    return fold_step


def laplace_inner(extended):
    return (
        extended[..., 2:, 1:-1]
        + extended[..., :-2, 1:-1]
        + extended[..., 1:-1, 2:]
        + extended[..., 1:-1, :-2]
        - 4.0 * extended[..., 1:-1, 1:-1]
    )


def clear_outside(extended, width, blk_index, axial):
    total_rows = axial * lax.axis_size("blk")
    rows_here = blk_index * axial - width + jnp.arange(axial + 2 * width, dtype=jnp.int32)
    inside = (rows_here >= 0) & (rows_here < total_rows)
    return jnp.where(inside[:, None], extended, 0.0)


def relax(motion, bend, load, stiffness, hoop_rows):
    half = motion.shape[0] // 2
    shift = hoop_spring * hoop_rows - inertia_term
    applied_re = bend[:half] - loss_factor * bend[half:] + shift * motion[:half]
    applied_im = bend[half:] + loss_factor * bend[:half] + shift * motion[half:]
    resid_re = load[:half] - applied_re
    resid_im = load[half:] - applied_im
    diag_re = 20.0 * stiffness + shift
    diag_im = 20.0 * loss_factor * stiffness
    denom = diag_re * diag_re + diag_im * diag_im
    update_re = (resid_re * diag_re + resid_im * diag_im) / denom
    update_im = (resid_im * diag_re - resid_re * diag_im) / denom
    return motion + relaxation * jnp.concatenate([update_re, update_im], axis=0)


def per_device(
    panels, node_of_panel, stiffener_rows, density_start, motion_start, force, stiffness
):
    panel_dev = panels.shape[1]
    channels = density_start.shape[0]
    axial, circum = stiffness.shape
    blk_index = lax.axis_index("blk")
    devices = lax.axis_size("blk") * lax.axis_size("circ")
    rows_global = blk_index * axial + jnp.arange(axial, dtype=jnp.int32)
    hoop_rows = jnp.any(rows_global[:, None] == stiffener_rows[None, :], axis=1).astype(
        jnp.float32
    )[:, None]
    panel_weight = panels[3] * (panel_dev * devices / (8.0 * math.pi))
    sources = lax.all_gather(panels, ("blk", "circ"), axis=1, tiled=True)
    target_rows = panels.shape[1]
    real_stack, imag_stack = form_kernels(panels, sources)
    fold_step = fold_columns(real_stack, imag_stack)
    density = density_start
    motion = motion_start
    pressure = jnp.zeros_like(density_start)
    for round_index in range(ITERS):
        flat_motion = motion.reshape(channels, axial * circum)
        neumann = jnp.take(flat_motion, node_of_panel, axis=1)
        density_bf = density.astype(jnp.bfloat16)
        start_sum = jnp.zeros((channels, 2 * target_rows), jnp.float32)
        combined = fold_step(
            start_sum, lax.all_gather(density_bf, ("blk", "circ"), axis=1, tiled=True), jnp.int32(0)
        )
        single_part = combined[:, :target_rows]
        double_part = combined[:, target_rows:]
        pressure = single_part
        density = 0.5 * density + neumann - double_part
        fluid = jnp.zeros((channels, axial * circum), jnp.float32)
        fluid = fluid.at[:, node_of_panel].add(panel_weight[None, :] * pressure)
        load = force - fluid.reshape(channels, axial, circum)
        for sweep_index in range(SWEEPS):
            motion_ext = padded(motion, (("blk", 1), ("circ", 2)), 1)
            motion_ext = clear_outside(motion_ext, 1, blk_index, axial)
            moment = stiffness * laplace_inner(motion_ext)
            moment_ext = padded(moment, (("blk", 1), ("circ", 2)), 1)
            moment_ext = clear_outside(moment_ext, 1, blk_index, axial)
            bend = laplace_inner(moment_ext)
            motion = relax(motion, bend, load, stiffness, hoop_rows)
    return (density, pressure, motion)


def solution(mesh):
    in_specs = (
        P(None, ("blk", "circ")),
        P(("blk", "circ")),
        P(),
        P(None, ("blk", "circ")),
        P(None, "blk", "circ"),
        P(None, "blk", "circ"),
        P("blk", "circ"),
    )
    out_specs = (P(None, ("blk", "circ")), P(None, ("blk", "circ")), P(None, "blk", "circ"))
    return jax.shard_map(
        per_device, mesh=mesh, in_specs=in_specs, out_specs=out_specs, check_vma=False
    )
```

profile of v0, /device:TPU:1, one launch (start us, length us, event | category | flops | bytes accessed | tf_op | source)
XLA Modules:
  0.0 2012.5 jit_solution(11817012427763911444)
XLA Ops:
  1.6 9.8 collective-permute-start.1
  13.5 347.8 %all-gather = f32[256,32,4]{1,2,0:T(4,128)S(1)} all-gather(f32[1,32,4]{1,2,0:T(4,128)S(1)} %bitcast.201), channel_id=1, replica_groups=mesh['blk'=64,'circ'=4] {'blk','circ'}, dimensions={0}, use_global_device_ids=true | all-gather | bytes 131584 | tf_op jit(solution)/shard_map/all_gather | solution.py:127
  361.7 11.7 while.15
  375.7 341.9 %all-gather.1 = bf16[256,32,16]{1,2,0:T(8,128)(2,1)S(1)} all-gather(bf16[1,32,16]{1,2,0:T(8,128)(2,1)S(1)} %convert_bitcast_fusion.3), channel_id=1, replica_groups=mesh['blk'=64,'circ'=4] {'blk','circ'}, dimensions={0}, use_global_device_ids=true | all-gather | bytes 263168 | tf_op jit(solution)/shard_map/all_gather | solution.py:140
  723.7 344.9 %all-gather.2 = bf16[256,32,16]{1,2,0:T(8,128)(2,1)S(1)} all-gather(bf16[1,32,16]{1,2,0:T(8,128)(2,1)S(1)} %get-tuple-element.276), channel_id=1, replica_groups=mesh['blk'=64,'circ'=4] {'blk','circ'}, dimensions={0}, use_global_device_ids=true | all-gather | bytes 263168 | tf_op jit(solution)/shard_map/all_gather | solution.py:140
  1079.9 4.0 collective-permute-done.3
  1087.1 4.3 collective-permute-done.4
  1101.7 4.8 collective-permute-done.8
  1117.6 4.3 collective-permute-done.12
  1131.9 4.3 collective-permute-done.16
  1149.2 4.0 collective-permute-done.20
  1163.2 349.0 %all-gather.3 = bf16[256,32,16]{1,2,0:T(8,128)(2,1)S(1)} all-gather(bf16[1,32,16]{1,2,0:T(8,128)(2,1)S(1)} %get-tuple-element.171), channel_id=1, replica_groups=mesh['blk'=64,'circ'=4] {'blk','circ'}, dimensions={0}, use_global_device_ids=true | all-gather | bytes 263168 | tf_op jit(solution)/shard_map/all_gather | solution.py:140
  1517.9 3.6 collective-permute-done.27
  1524.7 4.3 collective-permute-done.28
  1539.3 344.8 %all-gather.4 = bf16[256,32,16]{1,2,0:T(8,128)(2,1)S(1)} all-gather(bf16[1,32,16]{1,2,0:T(8,128)(2,1)S(1)} %get-tuple-element.274), channel_id=1, replica_groups=mesh['blk'=64,'circ'=4] {'blk','circ'}, dimensions={0}, use_global_device_ids=true | all-gather | bytes 263168 | tf_op jit(solution)/shard_map/all_gather | solution.py:140
  1890.0 4.3 collective-permute-done.32
  1908.7 3.6 collective-permute-start.39
  1921.2 4.5 collective-permute-done.40
  1931.4 3.8 collective-permute-done.43
  1938.4 4.3 collective-permute-done.44
  1952.3 4.7 collective-permute-done.48
  1968.6 4.3 collective-permute-done.52
  1983.7 4.3 collective-permute-done.56
  1999.3 4.3 collective-permute-done.60
  (363 shorter events, 200.2 us)
Async XLA Ops:
  1.6 1074.7 %collective-permute-start.1 = (f32[16,1,256]{2,1,0:T(1,128)S(1)}, f32[16,1,256]{2,1,0:T(1,128)S(1)}, u32[]{:S(2)}, u32[]{:S(2)}) collective-permute-start(f32[16,1,256]{2,1,0:T(1,128)S(1)} %get-tuple-element.272), channel_id=1, source_target_pairs={{4,0},{8,4},{12,8},{16,12},{20,16},{24,20},{28,24},{32,28},{36,32}... | collective-permute-start | bytes 49160 | tf_op jit(solution)/shard_map/ppermute | solution.py:27
  11.5 1064.9 %collective-permute-start = (f32[16,1,256]{2,1,0:T(1,128)S(1)}, f32[16,1,256]{2,1,0:T(1,128)S(1)}, u32[]{:S(2)}, u32[]{:S(2)}) collective-permute-start(f32[16,1,256]{2,1,0:T(1,128)S(1)} %get-tuple-element.271), channel_id=1, source_target_pairs={{0,4},{4,8},{8,12},{12,16},{16,20},{20,24},{24,28},{28,32},{32,36}... | collective-permute-start | bytes 49160 | tf_op jit(solution)/shard_map/ppermute | solution.py:24
  1076.5 7.3 collective-permute-start.3
  1076.8 7.1 collective-permute-start.2
  1084.5 6.9 collective-permute-start.4
  1099.3 7.2 collective-permute-start.8
  1106.6 7.8 collective-permute-start.11
  1115.1 6.9 collective-permute-start.12
  1129.3 6.9 collective-permute-start.16
  1136.4 8.9 collective-permute-start.19
  1161.7 352.7 %collective-permute-start.25 = (f32[16,1,256]{2,1,0:T(1,128)S(1)}, f32[16,1,256]{2,1,0:T(1,128)S(1)}, u32[]{:S(2)}, u32[]{:S(2)}) collective-permute-start(f32[16,1,256]{2,1,0:T(1,128)S(1)} %get-tuple-element.258), channel_id=1, source_target_pairs={{4,0},{8,4},{12,8},{16,12},{20,16},{24,20},{28,24},{32,28},{36,32}... | collective-permute-start | bytes 49160 | tf_op jit(solution)/shard_map/ppermute | solution.py:27
  1161.7 352.7 %collective-permute-start.24 = (f32[16,1,256]{2,1,0:T(1,128)S(1)}, f32[16,1,256]{2,1,0:T(1,128)S(1)}, u32[]{:S(2)}, u32[]{:S(2)}) collective-permute-start(f32[16,1,256]{2,1,0:T(1,128)S(1)} %get-tuple-element.257), channel_id=1, source_target_pairs={{0,4},{4,8},{8,12},{12,16},{16,20},{20,24},{24,28},{28,32},{32,36}... | collective-permute-start | bytes 49160 | tf_op jit(solution)/shard_map/ppermute | solution.py:24
  1514.6 6.9 collective-permute-start.27
  1522.2 6.9 collective-permute-start.28
  1887.4 6.9 collective-permute-start.32
  1901.6 6.9 collective-permute-start.36
  1908.7 9.2 collective-permute-start.39
  1925.9 9.3 collective-permute-start.43
  1935.9 6.9 collective-permute-start.44
  1957.1 8.2 collective-permute-start.51
  1966.0 6.9 collective-permute-start.52
  1973.0 7.2 collective-permute-start.55
  1988.1 8.0 collective-permute-start.59
  2003.8 7.2 collective-permute-start.63
  (59 other events, 3124.6 us)
where the time goes:
time: 2020 us; the launch traced here: 2010 us
  blocking collectives  1730 us (86%)
  waiting for transfers between devices  120 us (6%)
  starting transfers between devices  101 us (5%)
  other arithmetic  31.7 us (2%)
  local copies, waits for them, and re-layouts  24.9 us (1%)
    all_gather x4, blocking collectives, per_device(): lax.all_gather(density_bf, ('blk', 'circ'), axis=1, tiled=True)  1380 us
    all_gather x1, blocking collectives, per_device(): sources = lax.all_gather(panels, ('blk', 'circ'), axis=1, tiled=True)  348 us
    ppermute x32, waiting for transfers between devices, padded(): lax.ppermute(lax.slice_in_dim(block, 0, width, axis=dim), axis, backward)  61.1 us
    ppermute x32, waiting for transfers between devices, padded(): lax.ppermute(lax.slice_in_dim(block, block.shape[dim] - width, None, axis...  58.7 us
    ppermute x32, starting transfers between devices, padded(): lax.ppermute(lax.slice_in_dim(block, block.shape[dim] - width, None, axis...  53.5 us
    ppermute x32, starting transfers between devices, padded(): lax.ppermute(lax.slice_in_dim(block, 0, width, axis=dim), axis, backward)  47.8 us
  transfers between devices with their start and end apart: 64, of which 42 were waited for; matrix products, arithmetic and copies ran while one was open for 2% of the time, Pallas kernels for 0%

commit v1 on v0

--- a/solution.py
+++ b/solution.py
@@ -124,7 +124,10 @@
         jnp.float32
     )[:, None]
     panel_weight = panels[3] * (panel_dev * devices / (8.0 * math.pi))
-    sources = lax.all_gather(panels, ("blk", "circ"), axis=1, tiled=True)
+    sources = jnp.concatenate(
+        lax.all_to_all(jnp.stack([panels] * lax.axis_size(("blk", "circ"))), ("blk", "circ"), 0, 0),
+        axis=1,
+    )
     target_rows = panels.shape[1]
     real_stack, imag_stack = form_kernels(panels, sources)
     fold_step = fold_columns(real_stack, imag_stack)

time: 2020 us -> 1700 us (0.84)
  blocking collectives: 1730 us -> 1390 us
    all_gather x1 -> x0, blocking collectives: 348 us -> none  [per_device(): sources = lax.all_gather(panels, ('blk', 'circ'), axis=1, tiled=True)]
  transfers between devices with their start and end apart: 64 -> 65, of which waited for: 42 -> 42; matrix products, arithmetic and copies ran while one was open for 2% -> 1% of each run, Pallas kernels for 0% -> 0%
where the time goes in v1:
time: 1700 us; the launch traced here: 1690 us
  blocking collectives  1390 us (82%)
  waiting for transfers between devices  118 us (7%)
  starting transfers between devices  116 us (7%)
  other arithmetic  33.1 us (2%)
  local copies, waits for them, and re-layouts  25.8 us (2%)
    all_gather x4, blocking collectives, per_device(): lax.all_gather(density_bf, ('blk', 'circ'), axis=1, tiled=True)  1390 us
    ppermute x32, waiting for transfers between devices, padded(): lax.ppermute(lax.slice_in_dim(block, 0, width, axis=dim), axis, backward)  60.2 us
    ppermute x32, waiting for transfers between devices, padded(): lax.ppermute(lax.slice_in_dim(block, block.shape[dim] - width, None, axis...  57.7 us
    ppermute x32, starting transfers between devices, padded(): lax.ppermute(lax.slice_in_dim(block, block.shape[dim] - width, None, axis...  55.7 us
    ppermute x32, starting transfers between devices, padded(): lax.ppermute(lax.slice_in_dim(block, 0, width, axis=dim), axis, backward)  45 us
  transfers between devices with their start and end apart: 65, of which 42 were waited for; matrix products, arithmetic and copies ran while one was open for 1% of the time, Pallas kernels for 0%

profile of v1, /device:TPU:1, one launch (start us, length us, event | category | flops | bytes accessed | tf_op | source)
XLA Modules:
  0.0 1686.1 jit_solution(4721546688162398791)
XLA Ops:
  2.4 15.6 all-to-all-start
  18.1 7.6 collective-permute-start.1
  25.8 349.6 %all-gather = bf16[256,32,16]{1,2,0:T(8,128)(2,1)S(1)} all-gather(bf16[1,32,16]{1,2,0:T(8,128)(2,1)S(1)} %convert_bitcast_fusion.3), channel_id=1, replica_groups=mesh['blk'=64,'circ'=4] {'blk','circ'}, dimensions={0}, use_global_device_ids=true | all-gather | bytes 263168 | tf_op jit(solution)/shard_map/all_gather | solution.py:143
  382.5 3.6 collective-permute-done.3
  389.4 4.3 collective-permute-done.4
  404.1 11.7 while.15
  418.5 344.4 %all-gather.1 = bf16[256,32,16]{1,2,0:T(8,128)(2,1)S(1)} all-gather(bf16[1,32,16]{1,2,0:T(8,128)(2,1)S(1)} %get-tuple-element.276), channel_id=1, replica_groups=mesh['blk'=64,'circ'=4] {'blk','circ'}, dimensions={0}, use_global_device_ids=true | all-gather | bytes 263168 | tf_op jit(solution)/shard_map/all_gather | solution.py:143
  775.4 4.3 collective-permute-done.8
  789.8 4.3 collective-permute-done.12
  806.1 4.3 collective-permute-done.16
  822.1 4.0 collective-permute-done.20
  837.4 348.3 %all-gather.2 = bf16[256,32,16]{1,2,0:T(8,128)(2,1)S(1)} all-gather(bf16[1,32,16]{1,2,0:T(8,128)(2,1)S(1)} %get-tuple-element.171), channel_id=1, replica_groups=mesh['blk'=64,'circ'=4] {'blk','circ'}, dimensions={0}, use_global_device_ids=true | all-gather | bytes 263168 | tf_op jit(solution)/shard_map/all_gather | solution.py:143
  1191.4 3.6 collective-permute-done.27
  1198.2 4.3 collective-permute-done.28
  1213.2 344.2 %all-gather.3 = bf16[256,32,16]{1,2,0:T(8,128)(2,1)S(1)} all-gather(bf16[1,32,16]{1,2,0:T(8,128)(2,1)S(1)} %get-tuple-element.274), channel_id=1, replica_groups=mesh['blk'=64,'circ'=4] {'blk','circ'}, dimensions={0}, use_global_device_ids=true | all-gather | bytes 263168 | tf_op jit(solution)/shard_map/all_gather | solution.py:143
  1563.2 4.3 collective-permute-done.32
  1594.5 4.4 collective-permute-done.40
  1599.1 3.8 collective-permute-start.43
  1604.9 3.6 collective-permute-done.43
  1611.8 4.3 collective-permute-done.44
  1626.1 4.3 collective-permute-done.48
  1642.6 4.3 collective-permute-done.52
  1657.0 4.3 collective-permute-done.56
  1673.3 4.3 collective-permute-done.60
  (374 shorter events, 203.4 us)
Async XLA Ops:
  2.4 399.7 %all-to-all-start = ((f32[256,1,128]{2,1,0:T(1,128)}), f32[256,1,128]{2,1,0:T(1,128)S(1)}, u32[]{:S(2)}, u32[]{:S(2)}) async-start(f32[256,1,128]{2,1,0:T(1,128)} %reshape.1259), calls=%async_computation | async-start | bytes 262144 | tf_op jit(solution)/shard_map/all_to_all | solution.py:128
  18.1 360.9 %collective-permute-start.1 = (f32[16,1,256]{2,1,0:T(1,128)S(1)}, f32[16,1,256]{2,1,0:T(1,128)S(1)}, u32[]{:S(2)}, u32[]{:S(2)}) collective-permute-start(f32[16,1,256]{2,1,0:T(1,128)S(1)} %get-tuple-element.272), channel_id=1, source_target_pairs={{4,0},{8,4},{12,8},{16,12},{20,16},{24,20},{28,24},{32,28},{36,32}... | collective-permute-start | bytes 49160 | tf_op jit(solution)/shard_map/ppermute | solution.py:27
  25.7 353.3 %collective-permute-start = (f32[16,1,256]{2,1,0:T(1,128)S(1)}, f32[16,1,256]{2,1,0:T(1,128)S(1)}, u32[]{:S(2)}, u32[]{:S(2)}) collective-permute-start(f32[16,1,256]{2,1,0:T(1,128)S(1)} %get-tuple-element.271), channel_id=1, source_target_pairs={{0,4},{4,8},{8,12},{12,16},{16,20},{20,24},{24,28},{28,32},{32,36}... | collective-permute-start | bytes 49160 | tf_op jit(solution)/shard_map/ppermute | solution.py:24
  379.2 6.9 collective-permute-start.3
  386.8 6.9 collective-permute-start.4
  393.8 7.1 collective-permute-start.7
  772.8 6.9 collective-permute-start.8
  787.3 6.9 collective-permute-start.12
  794.3 8.4 collective-permute-start.15
  803.6 6.9 collective-permute-start.16
  810.6 7.6 collective-permute-start.19
  826.3 7.7 collective-permute-start.23
  835.4 352.4 %collective-permute-start.25 = (f32[16,1,256]{2,1,0:T(1,128)S(1)}, f32[16,1,256]{2,1,0:T(1,128)S(1)}, u32[]{:S(2)}, u32[]{:S(2)}) collective-permute-start(f32[16,1,256]{2,1,0:T(1,128)S(1)} %get-tuple-element.258), channel_id=1, source_target_pairs={{4,0},{8,4},{12,8},{16,12},{20,16},{24,20},{28,24},{32,28},{36,32}... | collective-permute-start | bytes 49160 | tf_op jit(solution)/shard_map/ppermute | solution.py:27
  835.9 351.9 %collective-permute-start.24 = (f32[16,1,256]{2,1,0:T(1,128)S(1)}, f32[16,1,256]{2,1,0:T(1,128)S(1)}, u32[]{:S(2)}, u32[]{:S(2)}) collective-permute-start(f32[16,1,256]{2,1,0:T(1,128)S(1)} %get-tuple-element.257), channel_id=1, source_target_pairs={{0,4},{4,8},{8,12},{12,16},{16,20},{20,24},{24,28},{28,32},{32,36}... | collective-permute-start | bytes 49160 | tf_op jit(solution)/shard_map/ppermute | solution.py:24
  1188.0 6.9 collective-permute-start.27
  1202.7 7.2 collective-permute-start.31
  1567.7 6.9 collective-permute-start.35
  1582.3 8.8 collective-permute-start.39
  1599.1 9.5 collective-permute-start.43
  1609.2 6.9 collective-permute-start.44
  1630.6 8.5 collective-permute-start.51
  1654.5 6.9 collective-permute-start.56
  1661.5 8.5 collective-permute-start.59
  1670.7 6.9 collective-permute-start.60
  (63 other events, 1419.7 us)
